TPU v7x, 512 devices: a whole 4x4x16 slice. The times are simulated.
512 devices in a mesh: head: 8 (over x, core), expert: 64 (over z, y).
Axes of the slice: x: 4, y: 4, z: 16, core: 2. Of those that a mesh axis runs over, the one named last changes fastest.
Arguments:
- q_latent: bfloat16 [512, 64, 512], P('expert', 'head'), may hold values from -16 to 16
- q_rotary: bfloat16 [512, 64, 64], P('expert', 'head'), may hold values from -3 to 3
- cache_latent: bfloat16 [512, 128, 512], P('expert'), may hold values from -5 to 5
- cache_rotary: bfloat16 [512, 64, 128], P('expert'), may hold values from -5 to 5
- lengths: int32 [512], P('expert'), may hold values from 16 to 128, as said below
- w_value_out: bfloat16 [32768, 5120], P('head', 'expert'), may hold values from -0.25 to 0.25
- resid: bfloat16 [512, 5120], P('expert'), may hold values from -8 to 8
- norm_gain: float32 [5120], replicated, may hold values from 0.1 to 1.9
- route_ids: int32 [512, 6], P('expert'), may hold values from 0 to 63, as said below
- route_weights: float32 [512, 6], P('expert'), may hold values from 0.1 to 0.6
- w_gate_up: bfloat16 [64, 2, 768, 5120], P('expert', None, 'head'), may hold values from -0.078125 to 0.078125
- w_down: bfloat16 [64, 768, 5120], P('expert', 'head'), may hold values from -0.21875 to 0.21875
Outputs:
- mixed_out: float32 [512, 5120], P('expert', 'head')
Inputs may be any that keep to these rules, and one draw needn't show every extreme that they name: `lengths`: slots at positions below a sequence's length are valid; some sequence has length 128. `route_ids`: each row names 6 different experts. Among the rows of one device (aligned blocks of 8 rows) no expert is named by more than 2 rows, and one expert is named by exactly 2 rows in every block.
All inputs are finite; a program needn't handle non-finite values.
Results may differ from a plain program's by a relative error of at most 0.0046.
Values may be sent and summed in bfloat16 or wider, within the bound.
No kernel may reach another device: no remote copies, remote signals or barrier semaphores. Data moves between devices by JAX's collectives and lax.ppermute only.
A program may use at most 64 MiB of HBM per device.

v0:
```python
import jax
import jax.numpy as jnp
from jax import lax
from jax.sharding import PartitionSpec as P

softmax_scale = 192.0 ** (-0.5)
norm_epsilon = 1e-06


def attend(q_latent, q_rotary, cache_latent, cache_rotary, lengths):
    scores = jnp.einsum("shl,scl->shc", q_latent, cache_latent, preferred_element_type=jnp.float32)
    scores = scores + jnp.einsum(
        "shr,src->shc", q_rotary, cache_rotary, preferred_element_type=jnp.float32
    )
    scores = scores * softmax_scale
    position = lax.broadcasted_iota(jnp.int32, scores.shape, 2)
    scores = jnp.where(position < lengths[:, None, None], scores, -1e30)
    highest = jnp.max(scores, axis=2, keepdims=True)
    weights = jnp.exp(scores - highest)
    probs = (weights / jnp.sum(weights, axis=2, keepdims=True)).astype(jnp.bfloat16)
    return jnp.einsum(
        "shc,scl->shl", probs, cache_latent, preferred_element_type=jnp.float32
    ).astype(jnp.bfloat16)


def on_device(
    q_latent,
    q_rotary,
    cache_latent,
    cache_rotary,
    lengths,
    w_value_out,
    resid,
    norm_gain,
    route_ids,
    route_weights,
    w_gate_up,
    w_down,
):
    seq_local = q_latent.shape[0]
    latent_out = attend(q_latent, q_rotary, cache_latent, cache_rotary, lengths)
    flattened = latent_out.reshape(seq_local, -1)
    column_terms = jnp.dot(
        lax.all_gather(flattened, "expert", axis=0, tiled=True),
        w_value_out,
        preferred_element_type=jnp.float32,
    )
    column_sums = lax.psum(column_terms, "head")
    attention = lax.all_to_all(
        column_sums.astype(jnp.bfloat16), "expert", split_axis=0, concat_axis=1, tiled=True
    )
    stream = resid.astype(jnp.float32) + attention.astype(jnp.float32)
    mean_square = jnp.mean(stream * stream, axis=1, keepdims=True)
    normed = (stream * lax.rsqrt(mean_square + norm_epsilon) * norm_gain).astype(jnp.bfloat16)
    expert_count = lax.axis_size("expert")
    top_count = route_ids.shape[1]
    capacity = max(2, -(-(seq_local * top_count) // expert_count))
    flat_ids = route_ids.reshape(-1)
    one_hot = (flat_ids[:, None] == jnp.arange(expert_count, dtype=jnp.int32)[None, :]).astype(
        jnp.int32
    )
    earlier = jnp.cumsum(one_hot, axis=0) - one_hot
    slot_index = jnp.sum(earlier * one_hot, axis=1)
    target = (flat_ids * capacity + slot_index).reshape(seq_local, top_count)
    places = jnp.arange(expert_count * capacity, dtype=jnp.int32)
    matches = target[None, :, :] == places[:, None, None]
    selector = jnp.sum(matches.astype(jnp.int32), axis=2).astype(jnp.bfloat16)
    blending = jnp.sum(jnp.where(matches, route_weights[None, :, :], 0.0), axis=2)
    gate_up = w_gate_up[0]
    down_local = w_down[0]
    col_width = stream.shape[1] // lax.axis_size("head")
    offset = lax.axis_index("head") * col_width
    normed_cols = lax.dynamic_slice_in_dim(normed, offset, col_width, 1)
    outgoing = jnp.dot(selector, normed_cols, preferred_element_type=jnp.float32).astype(
        jnp.bfloat16
    )
    outgoing = outgoing.reshape(expert_count, capacity, -1)
    arrived = lax.all_to_all(outgoing, "expert", split_axis=0, concat_axis=0, tiled=True)
    arrived_cols = arrived.reshape(-1, arrived.shape[2])
    flat_rows = lax.all_gather(arrived_cols, "head", axis=1, tiled=True)
    projected = jnp.einsum("rd,gfd->rgf", flat_rows, gate_up, preferred_element_type=jnp.float32)
    hidden = (jax.nn.silu(projected[:, 0]) * projected[:, 1]).astype(jnp.bfloat16)
    partial_rows = jnp.dot(hidden, down_local, preferred_element_type=jnp.float32)
    summed_cols = lax.psum_scatter(
        partial_rows.astype(jnp.bfloat16), "head", scatter_dimension=1, tiled=True
    )
    summed_rows = summed_cols.reshape(expert_count, capacity, -1)
    returned = lax.all_to_all(summed_rows, "expert", split_axis=0, concat_axis=0, tiled=True)
    back_rows = returned.reshape(expert_count * capacity, -1).astype(jnp.float32)
    mixture = jnp.dot(blending.T, back_rows, precision=lax.Precision.HIGHEST)
    stream_cols = lax.dynamic_slice_in_dim(stream, offset, col_width, 1)
    return stream_cols + mixture


def solution(mesh):
    placed = (
        P("expert", "head", None),
        P("expert", "head", None),
        P("expert", None, None),
        P("expert", None, None),
        P("expert"),
        P("head", "expert"),
        P("expert", None),
        P(),
        P("expert", None),
        P("expert", None),
        P("expert", None, "head", None),
        P("expert", "head", None),
    )
    return jax.shard_map(
        on_device, mesh=mesh, in_specs=placed, out_specs=P("expert", "head"), check_vma=False
    )
```

profile of v0, /device:TPU:7, one launch (start us, length us, event | category | flops | bytes accessed | tf_op | source)
XLA Modules:
  0.0 349.5 jit_solution(5322238232163485525)
XLA Ops:
  6.5 1.8 fusion.21
  8.3 1.1 fusion.8
  9.6 1.5 fusion.4
  11.1 0.7 copy.24
  12.3 142.5 %all-gather.3.cloned.1.call-done = bf16[512,4096]{1,0:T(8,128)(2,1)} async-done(((bf16[8,4096]{1,0:T(8,128)(2,1)}), bf16[512,4096]{1,0:T(8,128)(2,1)}) %all-gather.3.cloned.1.call-update) | async-done | bytes 4194320 | tf_op jit(solution)/shard_map/all_gather | solution.py:44
  154.8 3.6 %fusion.22 = f32[512,80]{0,1:T(8,128)S(1)} fusion(bf16[512,4096]{1,0:T(8,128)(2,1)} %all-gather.3.cloned.1.call-done, bf16[4096,80]{0,1:T(8,128)(2,1)S(1)} %copy-done.1), kind=kOutput, calls=%fused_computation.40 | convolution fusion | flops 335544320 | bytes 5013504 | tf_op jit(solution)/shard_map/dot_general | solution.py:43
  158.4 31.2 %all-reduce.1 = bf16[512,80]{0,1:T(8,128)(2,1)S(1)} all-reduce(f32[512,80]{0,1:T(8,128)S(1)} %fusion.22), channel_id=1, replica_groups=mesh['head'=8,'expert'=64] {'head'}, use_global_device_ids=true, to_apply=%region_2.3 | all-reduce | flops 40960 | bytes 245760 | tf_op jit(solution)/shard_map/psum | solution.py:48
  189.6 0.7 copy.18
  190.4 8.6 %all-to-all-start = ((bf16[64,8,80]{2,1,0:T(8,128)(2,1)}), bf16[64,8,80]{2,1,0:T(8,128)(2,1)S(1)}, u32[]{:S(2)}, u32[]{:S(2)}) async-start(bf16[64,8,80]{2,1,0:T(8,128)(2,1)} %bitcast), calls=%async_computation | async-start | bytes 262144 | tf_op jit(solution)/shard_map/all_to_all | solution.py:49
  199.1 0.8 dynamic-slice
  200.0 15.2 %all-to-all-done = bf16[64,8,80]{2,1,0:T(8,128)(2,1)S(1)} async-done(((bf16[64,8,80]{2,1,0:T(8,128)(2,1)}), bf16[64,8,80]{2,1,0:T(8,128)(2,1)S(1)}, u32[]{:S(2)}, u32[]{:S(2)}) %all-to-all-start) | async-done | bytes 81952 | tf_op jit(solution)/shard_map/all_to_all | solution.py:49
  215.6 0.3 convolution_convert_fusion.1
  216.0 20.6 %all_to_all.23 = bf16[64,2,640]{2,1,0:T(2,128)(2,1)S(1)} all-to-all(bf16[64,2,640]{2,1,0:T(2,128)(2,1)S(1)} %reshape.43), channel_id=1, replica_groups=mesh['head'=8,'expert'=64] {'expert'}, dimensions={0} | all-to-all | bytes 327680 | tf_op jit(solution)/shard_map/all_to_all | solution.py:78
  236.6 0.7 reshape.44
  237.4 24.3 %all-gather.5.cloned.1.call-done = bf16[128,5120]{1,0:T(8,128)(2,1)} async-done(((bf16[128,640]{1,0:T(8,128)(2,1)}), bf16[128,5120]{1,0:T(8,128)(2,1)}) %all-gather.5.cloned.1.call-update) | async-done | bytes 1310736 | tf_op jit(solution)/shard_map/all_gather | solution.py:80
  261.6 2.0 fusion.1
  263.6 1.7 convolution_convert_fusion
  265.4 1.5 copy.22
  266.9 40.3 %reduce-scatter.4.cloned.1.call-done = bf16[640,128]{1,0:T(8,128)(2,1)} async-done(((bf16[5120,128]{1,0:T(8,128)(2,1)}), bf16[640,128]{1,0:T(8,128)(2,1)}) %reduce-scatter.4.cloned.1.call-update) | async-done | bytes 163856
  307.2 1.1 copy.23
  308.2 0.7 reshape.45
  309.0 14.4 %all-to-all-start.2 = ((bf16[64,2,640]{2,1,0:T(2,128)(2,1)}), bf16[64,2,640]{2,1,0:T(2,128)(2,1)S(1)}, u32[]{:S(2)}, u32[]{:S(2)}) async-start(bf16[64,2,640]{2,1,0:T(2,128)(2,1)} %reshape.45), calls=%async_computation.2 | async-start | bytes 327680 | tf_op jit(solution)/shard_map/all_to_all | solution.py:88
  323.6 18.6 %all-to-all-done.2 = bf16[64,2,640]{2,1,0:T(2,128)(2,1)S(1)} async-done(((bf16[64,2,640]{2,1,0:T(2,128)(2,1)}), bf16[64,2,640]{2,1,0:T(2,128)(2,1)S(1)}, u32[]{:S(2)}, u32[]{:S(2)}) %all-to-all-start.2) | async-done | bytes 163872 | tf_op jit(solution)/shard_map/all_to_all | solution.py:88
  342.2 0.8 convolution_add_fusion.1
  (34 shorter events, 1.7 us)
Async XLA Ops:
  6.5 255.1 %copy-start = (bf16[1,2,96,5120]{3,2,1,0:T(8,128)(2,1)S(1)}, bf16[1,2,96,5120]{3,2,1,0:T(8,128)(2,1)}, u32[]{:S(2)}) copy-start(bf16[1,2,96,5120]{3,2,1,0:T(8,128)(2,1)} %param.22) | copy-start | bytes 5898244
  6.5 5.3 %copy-start.3 = (s32[8,6]{1,0:T(8,128)S(1)}, s32[8,6]{1,0:T(8,128)}, u32[]{:S(2)}) copy-start(s32[8,6]{1,0:T(8,128)} %param.20) | copy-start | bytes 580
  6.5 148.3 %copy-start.1 = (bf16[4096,80]{0,1:T(8,128)(2,1)S(1)}, bf16[4096,80]{0,1:T(8,128)(2,1)}, u32[]{:S(2)}) copy-start(bf16[4096,80]{0,1:T(8,128)(2,1)} %param.17) | copy-start | bytes 1966084
  6.5 148.3 %all-gather.3.cloned.1.call-start = ((), (), s32[]{:S(2)}) async-start(), calls=%async_computation.4 | async-start | bytes 4259840 | tf_op jit(solution)/shard_map/all_gather | solution.py:44
  158.4 57.0 %copy-start.2 = (bf16[8,5120]{1,0:T(8,128)(2,1)S(1)}, bf16[8,5120]{1,0:T(8,128)(2,1)}, u32[]{:S(2)}) copy-start(bf16[8,5120]{1,0:T(8,128)(2,1)} %param.18) | copy-start | bytes 245764
  190.4 24.8 %all-to-all-start = ((bf16[64,8,80]{2,1,0:T(8,128)(2,1)}), bf16[64,8,80]{2,1,0:T(8,128)(2,1)S(1)}, u32[]{:S(2)}, u32[]{:S(2)}) async-start(bf16[64,8,80]{2,1,0:T(8,128)(2,1)} %bitcast), calls=%async_computation | async-start | bytes 262144 | tf_op jit(solution)/shard_map/all_to_all | solution.py:49
  199.0 62.6 %all-gather.5.cloned.1.call-start = ((), (), s32[]{:S(2)}) async-start(), calls=%async_computation.5 | async-start | bytes 1474560 | tf_op jit(solution)/shard_map/all_gather | solution.py:80
  237.3 69.9 %reduce-scatter.4.cloned.1.call-start = ((), (), s32[]{:S(2)}) async-start(), calls=%async_computation.6 | async-start | bytes 1474560
  265.4 58.0 %copy-start.4 = (f32[8,6]{1,0:T(8,128)S(1)}, f32[8,6]{1,0:T(8,128)}, u32[]{:S(2)}) copy-start(f32[8,6]{1,0:T(8,128)} %param.21) | copy-start | bytes 580
  309.0 33.2 %all-to-all-start.2 = ((bf16[64,2,640]{2,1,0:T(2,128)(2,1)}), bf16[64,2,640]{2,1,0:T(2,128)(2,1)S(1)}, u32[]{:S(2)}, u32[]{:S(2)}) async-start(bf16[64,2,640]{2,1,0:T(2,128)(2,1)} %reshape.45), calls=%async_computation.2 | async-start | bytes 327680 | tf_op jit(solution)/shard_map/all_to_all | solution.py:88
Sparse Core Ops, SparseCore 0:
  11.9 142.8 all-gather.2
  237.4 24.1 all-gather.4
  267.0 40.1 reduce-scatter.3
where the time goes:
time: 350 us
  waiting for transfers between devices  241 us (69%)
  blocking collectives  51.8 us (15%)
  starting transfers between devices  23.1 us (7%)
  between operations  13.2 us (4%)
  matrix products  12.8 us (4%)
  local copies, waits for them, and re-layouts  6.85 us (2%)
    all_gather x1, waiting for transfers between devices, on_device(): lax.all_gather(flattened, 'expert', axis=0, tiled=True)  143 us
    unnamed x4, waiting for transfers between devices  40.4 us
    psum x1, blocking collectives, on_device(): column_sums = lax.psum(column_terms, 'head')  31.2 us
    all_gather x1, waiting for transfers between devices, on_device(): flat_rows = lax.all_gather(arrived_cols, 'head', axis=1, tiled=True)  24.3 us
    all_to_all x1, blocking collectives, on_device(): lax.all_to_all(outgoing, 'expert', split_axis=0, concat_axis=0, tiled=True)  20.6 us
    all_to_all x1, waiting for transfers between devices, on_device(): lax.all_to_all(summed_rows, 'expert', split_axis=0, concat_axis=0, tiled=...  18.6 us
    all_to_all x1, waiting for transfers between devices, on_device(): lax.all_to_all(column_sums.astype(jnp.bfloat16), 'expert', split_axis=0,...  15.2 us
    all_to_all x1, starting transfers between devices, on_device(): lax.all_to_all(summed_rows, 'expert', split_axis=0, concat_axis=0, tiled=...  14.4 us
  transfers between devices with their start and end apart: 5, of which 5 were waited for; matrix products, arithmetic and copies ran while one was open for 0% of the time, Pallas kernels for 0%

commit v1 on v0

--- a/solution.py
+++ b/solution.py
@@ -5,6 +5,22 @@
 
 softmax_scale = 192.0 ** (-0.5)
 norm_epsilon = 1e-06
+
+
+def ring_product(x, axis, dim, term):
+    length, index, span = (lax.axis_size(axis), lax.axis_index(axis), x.shape[dim])
+    right = [(i, (i + 1) % length) for i in range(length)]
+    left = [(i, (i - 1) % length) for i in range(length)]
+    half = length // 2
+    from_left = from_right = x
+    total = term(x, index * span)
+    for hop in range(1, half + 1):
+        from_left = lax.ppermute(from_left, axis, right)
+        if hop < length - half:
+            from_right = lax.ppermute(from_right, axis, left)
+            total = total + term(from_right, (index + hop) % length * span)
+        total = total + term(from_left, (index - hop) % length * span)
+    return total
 
 
 def attend(q_latent, q_rotary, cache_latent, cache_rotary, lengths):
@@ -77,8 +93,17 @@
     outgoing = outgoing.reshape(expert_count, capacity, -1)
     arrived = lax.all_to_all(outgoing, "expert", split_axis=0, concat_axis=0, tiled=True)
     arrived_cols = arrived.reshape(-1, arrived.shape[2])
-    flat_rows = lax.all_gather(arrived_cols, "head", axis=1, tiled=True)
-    projected = jnp.einsum("rd,gfd->rgf", flat_rows, gate_up, preferred_element_type=jnp.float32)
+    projected = ring_product(
+        arrived_cols,
+        "head",
+        1,
+        lambda part, start: jnp.einsum(
+            "rd,gfd->rgf",
+            part,
+            lax.dynamic_slice_in_dim(gate_up, start, part.shape[1], axis=2),
+            preferred_element_type=jnp.float32,
+        ),
+    )
     hidden = (jax.nn.silu(projected[:, 0]) * projected[:, 1]).astype(jnp.bfloat16)
     partial_rows = jnp.dot(hidden, down_local, preferred_element_type=jnp.float32)
     summed_cols = lax.psum_scatter(

time: 350 us -> 339 us (0.969)
  starting transfers between devices: 23.1 us -> 43.8 us
  blocking collectives: 51.8 us -> 31.2 us
  waiting for transfers between devices: 241 us -> 231 us
    all_gather x1 -> x0, waiting for transfers between devices: 24.3 us -> none  [on_device(): flat_rows = lax.all_gather(arrived_cols, 'head', axis=1, tiled=True)]
    all_to_all x1 -> x0, blocking collectives: 20.6 us -> none  [on_device(): lax.all_to_all(outgoing, 'expert', split_axis=0, concat_axis=0, tiled=True)]
    all_to_all x0 -> x1, waiting for transfers between devices: none -> 15.6 us  [on_device(): lax.all_to_all(outgoing, 'expert', split_axis=0, concat_axis=0, tiled=True)]
    ppermute x0 -> x7, starting transfers between devices: none -> 15.3 us  [the longest x4 11.1 us: ring_product(): from_left = lax.ppermute(from_left, axis, right)]
    unnamed x4 -> x3, waiting for transfers between devices: 40.4 us -> 31.5 us
    ppermute x0 -> x7, waiting for transfers between devices: none -> 7.3 us  [the longest x4 7.28 us: ring_product(): from_left = lax.ppermute(from_left, axis, right)]
    all_to_all x0 -> x1, starting transfers between devices: none -> 5.43 us  [on_device(): lax.all_to_all(outgoing, 'expert', split_axis=0, concat_axis=0, tiled=True)]
  transfers between devices with their start and end apart: 5 -> 12, of which waited for: 5 -> 9; matrix products, arithmetic and copies ran while one was open for 0% -> 1% of each run, Pallas kernels for 0% -> 0%
where the time goes in v1:
time: 339 us
  waiting for transfers between devices  231 us (68%)
  starting transfers between devices  43.8 us (13%)
  blocking collectives  31.2 us (9%)
  between operations  13.8 us (4%)
  matrix products  11.4 us (3%)
  local copies, waits for them, and re-layouts  6.91 us (2%)
    all_gather x1, waiting for transfers between devices, on_device(): lax.all_gather(flattened, 'expert', axis=0, tiled=True)  143 us
    unnamed x3, waiting for transfers between devices  31.5 us
    psum x1, blocking collectives, on_device(): column_sums = lax.psum(column_terms, 'head')  31.2 us
    all_to_all x1, waiting for transfers between devices, on_device(): lax.all_to_all(summed_rows, 'expert', split_axis=0, concat_axis=0, tiled=...  18.5 us
    all_to_all x1, waiting for transfers between devices, on_device(): lax.all_to_all(outgoing, 'expert', split_axis=0, concat_axis=0, tiled=True)  15.6 us
    all_to_all x1, waiting for transfers between devices, on_device(): lax.all_to_all(column_sums.astype(jnp.bfloat16), 'expert', split_axis=0,...  15.2 us
    all_to_all x1, starting transfers between devices, on_device(): lax.all_to_all(summed_rows, 'expert', split_axis=0, concat_axis=0, tiled=...  14.4 us
    ppermute x4, starting transfers between devices, ring_product(): from_left = lax.ppermute(from_left, axis, right)  11.1 us
  transfers between devices with their start and end apart: 12, of which 9 were waited for; matrix products, arithmetic and copies ran while one was open for 1% of the time, Pallas kernels for 0%

profile of v1, /device:TPU:7, one launch (start us, length us, event | category | flops | bytes accessed | tf_op | source)
XLA Modules:
  0.0 338.6 jit_solution(9450689252572971010)
XLA Ops:
  6.5 1.8 fusion.54
  8.3 1.1 fusion.7
  9.6 1.5 fusion.3
  12.3 142.5 %all-gather.2.cloned.1.call-done = bf16[512,4096]{1,0:T(8,128)(2,1)} async-done(((bf16[8,4096]{1,0:T(8,128)(2,1)}), bf16[512,4096]{1,0:T(8,128)(2,1)}) %all-gather.2.cloned.1.call-update) | async-done | bytes 4194320 | tf_op jit(solution)/shard_map/all_gather | solution.py:60
  154.8 3.6 %fusion.55 = f32[512,80]{0,1:T(8,128)S(1)} fusion(bf16[512,4096]{1,0:T(8,128)(2,1)} %all-gather.2.cloned.1.call-done, bf16[4096,80]{0,1:T(8,128)(2,1)S(1)} %copy-done.2), kind=kOutput, calls=%fused_computation.78 | convolution fusion | flops 335544320 | bytes 5013504 | tf_op jit(solution)/shard_map/dot_general | solution.py:59
  158.4 31.2 %all-reduce.1 = bf16[512,80]{0,1:T(8,128)(2,1)S(1)} all-reduce(f32[512,80]{0,1:T(8,128)S(1)} %fusion.55), channel_id=1, replica_groups=mesh['head'=8,'expert'=64] {'head'}, use_global_device_ids=true, to_apply=%region_2.3 | all-reduce | flops 40960 | bytes 245760 | tf_op jit(solution)/shard_map/psum | solution.py:64
  190.4 8.6 %all-to-all-start = ((bf16[64,8,80]{2,1,0:T(8,128)(2,1)}), bf16[64,8,80]{2,1,0:T(8,128)(2,1)S(1)}, u32[]{:S(2)}, u32[]{:S(2)}) async-start(bf16[64,8,80]{2,1,0:T(8,128)(2,1)} %bitcast), calls=%async_computation | async-start | bytes 262144 | tf_op jit(solution)/shard_map/all_to_all | solution.py:65
  199.9 15.2 %all-to-all-done = bf16[64,8,80]{2,1,0:T(8,128)(2,1)S(1)} async-done(((bf16[64,8,80]{2,1,0:T(8,128)(2,1)}), bf16[64,8,80]{2,1,0:T(8,128)(2,1)S(1)}, u32[]{:S(2)}, u32[]{:S(2)}) %all-to-all-start) | async-done | bytes 81952 | tf_op jit(solution)/shard_map/all_to_all | solution.py:65
  216.6 5.4 %all-to-all-start.1 = ((bf16[64,2,640]{2,1,0:T(2,128)(2,1)}), bf16[64,2,640]{2,1,0:T(2,128)(2,1)S(1)}, u32[]{:S(2)}, u32[]{:S(2)}) async-start(bf16[64,2,640]{2,1,0:T(2,128)(2,1)} %reshape.51), calls=%async_computation.1 | async-start | bytes 327680 | tf_op jit(solution)/shard_map/all_to_all | solution.py:94
  222.2 15.6 %all-to-all-done.1 = bf16[64,2,640]{2,1,0:T(2,128)(2,1)S(1)} async-done(((bf16[64,2,640]{2,1,0:T(2,128)(2,1)}), bf16[64,2,640]{2,1,0:T(2,128)(2,1)S(1)}, u32[]{:S(2)}, u32[]{:S(2)}) %all-to-all-start.1) | async-done | bytes 163872 | tf_op jit(solution)/shard_map/all_to_all | solution.py:94
  237.9 4.2 %collective-permute-start = (bf16[128,640]{1,0:T(8,128)(2,1)S(1)}, bf16[128,640]{1,0:T(8,128)(2,1)S(1)}, u32[]{:S(2)}, u32[]{:S(2)}) collective-permute-start(bf16[128,640]{1,0:T(8,128)(2,1)S(1)} %reshape.52), channel_id=1, source_target_pairs={{0,448},{64,0},{128,64},{192,128},{256,192},{320,256},{384,320},{4... | collective-permute-start | bytes 491528 | tf_op jit(solution)/shard_map/ppermute | solution.py:20
  242.4 2.0 collective-permute-done.1
  244.4 3.7 %collective-permute-start.3 = (bf16[128,640]{1,0:T(8,128)(2,1)S(1)}, bf16[128,640]{1,0:T(8,128)(2,1)S(1)}, u32[]{:S(2)}, u32[]{:S(2)}) collective-permute-start(bf16[128,640]{1,0:T(8,128)(2,1)S(1)} %collective-permute-done.1), channel_id=1, source_target_pairs={{0,64},{64,128},{128,192},{192,256},{256,320},{320,384},{384,448},... | collective-permute-start | bytes 491528 | tf_op jit(solution)/shard_map/ppermute | solution.py:18
  248.5 1.8 collective-permute-done.3
  250.3 3.7 %collective-permute-start.5 = (bf16[128,640]{1,0:T(8,128)(2,1)S(1)}, bf16[128,640]{1,0:T(8,128)(2,1)S(1)}, u32[]{:S(2)}, u32[]{:S(2)}) collective-permute-start(bf16[128,640]{1,0:T(8,128)(2,1)S(1)} %collective-permute-done.3), channel_id=1, source_target_pairs={{0,64},{64,128},{128,192},{192,256},{256,320},{320,384},{384,448},... | collective-permute-start | bytes 491528 | tf_op jit(solution)/shard_map/ppermute | solution.py:18
  254.5 1.8 collective-permute-done.5
  256.3 3.7 %collective-permute-start.6 = (bf16[128,640]{1,0:T(8,128)(2,1)S(1)}, bf16[128,640]{1,0:T(8,128)(2,1)S(1)}, u32[]{:S(2)}, u32[]{:S(2)}) collective-permute-start(bf16[128,640]{1,0:T(8,128)(2,1)S(1)} %collective-permute-done.5), channel_id=1, source_target_pairs={{0,64},{64,128},{128,192},{192,256},{256,320},{320,384},{384,448},... | collective-permute-start | bytes 491528 | tf_op jit(solution)/shard_map/ppermute | solution.py:18
  260.5 1.8 collective-permute-done.6
  263.0 1.5 copy.22
  264.5 31.5 %reduce-scatter.4.cloned.1.call-done = bf16[640,128]{1,0:T(8,128)(2,1)} async-done(((bf16[5120,128]{1,0:T(8,128)(2,1)}), bf16[640,128]{1,0:T(8,128)(2,1)}) %reduce-scatter.4.cloned.1.call-update) | async-done | bytes 163856
  296.0 1.1 copy.23
  297.8 14.4 %all-to-all-start.2 = ((bf16[64,2,640]{2,1,0:T(2,128)(2,1)}), bf16[64,2,640]{2,1,0:T(2,128)(2,1)S(1)}, u32[]{:S(2)}, u32[]{:S(2)}) async-start(bf16[64,2,640]{2,1,0:T(2,128)(2,1)} %reshape.53), calls=%async_computation.2 | async-start | bytes 327680 | tf_op jit(solution)/shard_map/all_to_all | solution.py:113
  312.4 18.5 %all-to-all-done.2 = bf16[64,2,640]{2,1,0:T(2,128)(2,1)S(1)} async-done(((bf16[64,2,640]{2,1,0:T(2,128)(2,1)}), bf16[64,2,640]{2,1,0:T(2,128)(2,1)S(1)}, u32[]{:S(2)}, u32[]{:S(2)}) %all-to-all-start.2) | async-done | bytes 163872 | tf_op jit(solution)/shard_map/all_to_all | solution.py:113
  331.0 0.8 convolution_add_fusion.6
  (56 shorter events, 8.0 us)
Async XLA Ops:
  6.5 235.6 %copy-start = (bf16[1,2,96,5120]{3,2,1,0:T(8,128)(2,1)S(1)}, bf16[1,2,96,5120]{3,2,1,0:T(8,128)(2,1)}, u32[]{:S(2)}) copy-start(bf16[1,2,96,5120]{3,2,1,0:T(8,128)(2,1)} %param.22) | copy-start | bytes 5898244
  6.5 5.3 %copy-start.4 = (s32[8,6]{1,0:T(8,128)S(1)}, s32[8,6]{1,0:T(8,128)}, u32[]{:S(2)}) copy-start(s32[8,6]{1,0:T(8,128)} %param.20) | copy-start | bytes 580
  6.5 148.3 %copy-start.2 = (bf16[4096,80]{0,1:T(8,128)(2,1)S(1)}, bf16[4096,80]{0,1:T(8,128)(2,1)}, u32[]{:S(2)}) copy-start(bf16[4096,80]{0,1:T(8,128)(2,1)} %param.17) | copy-start | bytes 1966084
  6.5 148.3 %all-gather.2.cloned.1.call-start = ((), (), s32[]{:S(2)}) async-start(), calls=%async_computation.4 | async-start | bytes 4259840 | tf_op jit(solution)/shard_map/all_gather | solution.py:60
  158.4 57.0 %copy-start.3 = (bf16[8,5120]{1,0:T(8,128)(2,1)S(1)}, bf16[8,5120]{1,0:T(8,128)(2,1)}, u32[]{:S(2)}) copy-start(bf16[8,5120]{1,0:T(8,128)(2,1)} %param.18) | copy-start | bytes 245764
  190.4 24.8 %all-to-all-start = ((bf16[64,8,80]{2,1,0:T(8,128)(2,1)}), bf16[64,8,80]{2,1,0:T(8,128)(2,1)S(1)}, u32[]{:S(2)}, u32[]{:S(2)}) async-start(bf16[64,8,80]{2,1,0:T(8,128)(2,1)} %bitcast), calls=%async_computation | async-start | bytes 262144 | tf_op jit(solution)/shard_map/all_to_all | solution.py:65
  216.6 21.2 %all-to-all-start.1 = ((bf16[64,2,640]{2,1,0:T(2,128)(2,1)}), bf16[64,2,640]{2,1,0:T(2,128)(2,1)S(1)}, u32[]{:S(2)}, u32[]{:S(2)}) async-start(bf16[64,2,640]{2,1,0:T(2,128)(2,1)} %reshape.51), calls=%async_computation.1 | async-start | bytes 327680 | tf_op jit(solution)/shard_map/all_to_all | solution.py:94
  222.0 73.9 %reduce-scatter.4.cloned.1.call-start = ((), (), s32[]{:S(2)}) async-start(), calls=%async_computation.5 | async-start | bytes 1474560
  237.9 10.2 %collective-permute-start = (bf16[128,640]{1,0:T(8,128)(2,1)S(1)}, bf16[128,640]{1,0:T(8,128)(2,1)S(1)}, u32[]{:S(2)}, u32[]{:S(2)}) collective-permute-start(bf16[128,640]{1,0:T(8,128)(2,1)S(1)} %reshape.52), channel_id=1, source_target_pairs={{0,448},{64,0},{128,64},{192,128},{256,192},{320,256},{384,320},{4... | collective-permute-start | bytes 491528 | tf_op jit(solution)/shard_map/ppermute | solution.py:20
  242.1 2.3 collective-permute-start.1
  244.4 6.0 %collective-permute-start.3 = (bf16[128,640]{1,0:T(8,128)(2,1)S(1)}, bf16[128,640]{1,0:T(8,128)(2,1)S(1)}, u32[]{:S(2)}, u32[]{:S(2)}) collective-permute-start(bf16[128,640]{1,0:T(8,128)(2,1)S(1)} %collective-permute-done.1), channel_id=1, source_target_pairs={{0,64},{64,128},{128,192},{192,256},{256,320},{320,384},{384,448},... | collective-permute-start | bytes 491528 | tf_op jit(solution)/shard_map/ppermute | solution.py:18
  248.1 6.2 %collective-permute-start.2 = (bf16[128,640]{1,0:T(8,128)(2,1)S(1)}, bf16[128,640]{1,0:T(8,128)(2,1)S(1)}, u32[]{:S(2)}, u32[]{:S(2)}) collective-permute-start(bf16[128,640]{1,0:T(8,128)(2,1)S(1)} %collective-permute-done), channel_id=1, source_target_pairs={{0,448},{64,0},{128,64},{192,128},{256,192},{320,256},{384,320},{4... | collective-permute-start | bytes 491528 | tf_op jit(solution)/shard_map/ppermute | solution.py:20
  248.3 14.2 %copy-start.1 = (bf16[1,96,5120]{2,1,0:T(8,128)(2,1)S(1)}, bf16[1,96,5120]{2,1,0:T(8,128)(2,1)}, u32[]{:S(2)}) copy-start(bf16[1,96,5120]{2,1,0:T(8,128)(2,1)} %param.23) | copy-start | bytes 2949124
  250.3 6.0 %collective-permute-start.5 = (bf16[128,640]{1,0:T(8,128)(2,1)S(1)}, bf16[128,640]{1,0:T(8,128)(2,1)S(1)}, u32[]{:S(2)}, u32[]{:S(2)}) collective-permute-start(bf16[128,640]{1,0:T(8,128)(2,1)S(1)} %collective-permute-done.3), channel_id=1, source_target_pairs={{0,64},{64,128},{128,192},{192,256},{256,320},{320,384},{384,448},... | collective-permute-start | bytes 491528 | tf_op jit(solution)/shard_map/ppermute | solution.py:18
  254.3 6.0 %collective-permute-start.4 = (bf16[128,640]{1,0:T(8,128)(2,1)S(1)}, bf16[128,640]{1,0:T(8,128)(2,1)S(1)}, u32[]{:S(2)}, u32[]{:S(2)}) collective-permute-start(bf16[128,640]{1,0:T(8,128)(2,1)S(1)} %collective-permute-done.2), channel_id=1, source_target_pairs={{0,448},{64,0},{128,64},{192,128},{256,192},{320,256},{384,320},{4... | collective-permute-start | bytes 491528 | tf_op jit(solution)/shard_map/ppermute | solution.py:20
  256.3 6.0 %collective-permute-start.6 = (bf16[128,640]{1,0:T(8,128)(2,1)S(1)}, bf16[128,640]{1,0:T(8,128)(2,1)S(1)}, u32[]{:S(2)}, u32[]{:S(2)}) collective-permute-start(bf16[128,640]{1,0:T(8,128)(2,1)S(1)} %collective-permute-done.5), channel_id=1, source_target_pairs={{0,64},{64,128},{128,192},{192,256},{256,320},{320,384},{384,448},... | collective-permute-start | bytes 491528 | tf_op jit(solution)/shard_map/ppermute | solution.py:18
  263.0 49.2 %copy-start.5 = (f32[8,6]{1,0:T(8,128)S(1)}, f32[8,6]{1,0:T(8,128)}, u32[]{:S(2)}) copy-start(f32[8,6]{1,0:T(8,128)} %param.21) | copy-start | bytes 580
  297.8 33.1 %all-to-all-start.2 = ((bf16[64,2,640]{2,1,0:T(2,128)(2,1)}), bf16[64,2,640]{2,1,0:T(2,128)(2,1)S(1)}, u32[]{:S(2)}, u32[]{:S(2)}) async-start(bf16[64,2,640]{2,1,0:T(2,128)(2,1)} %reshape.53), calls=%async_computation.2 | async-start | bytes 327680 | tf_op jit(solution)/shard_map/all_to_all | solution.py:113
Sparse Core Ops, SparseCore 0:
  11.9 142.8 all-gather.1
  264.6 31.3 reduce-scatter.3
